TPU v7x, 32 devices: a whole 2x2x4 slice. The times are simulated.
32 devices in a mesh: walk: 4 (over x, core), chol: 8 (over z, y).
Axes of the slice: x: 2, y: 2, z: 4, core: 2. Of those that a mesh axis runs over, the one named last changes fastest.
Arguments:
- old_walkers: bfloat16 [96, 2048, 128], P(('walk', 'chol'))
- half_chol: bfloat16 [16, 128, 2048], P('chol'), may hold values from -0.1875 to 0.1875
- parent: int32 [192], P(('walk', 'chol')), may hold values from -1 to 11, as said below
- field: float32 [192, 2048], P(('walk', 'chol')), may hold values from -0.8 to 0.8
Outputs:
- new_walkers: bfloat16 [192, 2048, 128], P(('walk', 'chol'))
- energy: float32 [192], P(('walk', 'chol'))
Inputs may be any that keep to these rules, and one draw needn't show every extreme that they name: `parent`: the 4 devices that share an index of chol form a column. On each device the live slots (value >= 0) come first among its 6 slots, the rest hold -1. Each column has exactly 12 live slots, every device of it at least one, and some device of it has all 6 slots live. A live value m names the walker that the column's walk index m // 3 holds as its local walker m % 3.
All inputs are finite; a program needn't handle non-finite values.
Results may differ from a plain program's by a relative error of at most 0.0062.
Values may be sent and summed in bfloat16 or wider, within the bound.
No kernel may reach another device: no remote copies, remote signals or barrier semaphores. Data moves between devices by JAX's collectives and lax.ppermute only.
A program may use at most 192 MiB of HBM per device.

v0:
```python
import jax
import jax.numpy as jnp
from jax import lax
from jax.sharding import PartitionSpec as P

ITERS = 3


def green_half(walkers):
    widened = walkers.astype(jnp.float32)
    electrons = walkers.shape[2]
    intersection = widened[:, :electrons, :]
    identity = jnp.eye(electrons, dtype=jnp.float32)
    diagonal = jnp.diagonal(intersection, axis1=1, axis2=2)
    inverse = identity[None, :, :] / diagonal[:, None, :]
    for sweep in range(ITERS):
        product = jnp.einsum("wij,wjk->wik", intersection, inverse, precision=lax.Precision.HIGHEST)
        inverse = jnp.einsum(
            "wij,wjk->wik",
            inverse,
            2.0 * identity[None, :, :] - product,
            precision=lax.Precision.HIGHEST,
        )
    theta = jnp.einsum("wnk,wkj->wnj", widened, inverse, precision=lax.Precision.HIGHEST)
    return theta.astype(jnp.bfloat16)


def block_energy(theta, vectors):
    blocks = jnp.einsum("gin,wnj->wgij", vectors, theta, preferred_element_type=jnp.float32)
    traces = jnp.einsum("wgii->wg", blocks)
    crossed = jnp.sum(blocks * jnp.swapaxes(blocks, 2, 3), axis=(2, 3))
    return 0.5 * jnp.sum(traces * traces - crossed, axis=1)


def swap_pairs(x, axis, size, bit):
    perm = [(i, i ^ bit) for i in range(size)]
    return lax.ppermute(x, axis, perm)


def body(old_walkers, half_chol, parent, field):
    n_walk = lax.axis_size("walk")
    old_dev = old_walkers.shape[0]
    slot_dev = parent.shape[0]
    walk_id = lax.axis_index("walk")
    core = walk_id % 2
    local_g = half_chol.shape[0]
    half_g = local_g // 2
    mine = lax.dynamic_slice_in_dim(half_chol, core * half_g, half_g, axis=0)
    gathered = lax.all_gather(mine, "chol", axis=0, tiled=True)
    other = swap_pairs(gathered, "walk", n_walk, 1)
    across = swap_pairs(old_walkers, "walk", n_walk, 2)
    beside = swap_pairs(old_walkers, "walk", n_walk, 1)
    diagonal_peer = swap_pairs(across, "walk", n_walk, 1)
    column = jnp.concatenate([old_walkers, beside, across, diagonal_peer], axis=0)
    living = parent >= 0
    source = jnp.maximum(parent, 0)
    relative = source // old_dev ^ walk_id
    index = relative * old_dev + source % old_dev
    kicked = (jnp.exp(field)[:, :, None] * column[index].astype(jnp.float32)).astype(jnp.bfloat16)
    new_walkers = jnp.where(living[:, None, None], kicked, jnp.zeros_like(kicked))
    theta = green_half(kicked)
    energy = block_energy(theta, gathered) + block_energy(theta, other)
    energy = jnp.where(living, energy, 0.0)
    return (new_walkers, energy)


def solution(mesh):
    return jax.shard_map(
        body,
        mesh=mesh,
        in_specs=(
            P(("walk", "chol"), None, None),
            P("chol", None, None),
            P(("walk", "chol")),
            P(("walk", "chol"), None),
        ),
        out_specs=(P(("walk", "chol"), None, None), P(("walk", "chol"))),
        check_vma=False,
    )
```

profile of v0, /device:TPU:1, one launch (start us, length us, event | category | flops | bytes accessed | tf_op | source)
XLA Modules:
  0.0 153.9 jit_solution(10622074899993358610)
XLA Ops:
  7.2 1.2 copy-done
  8.4 0.8 constant_dynamic-slice_fusion
  9.3 2.1 %collective-permute-start.1 = (bf16[3,2048,128]{2,1,0:T(8,128)(2,1)}, bf16[3,2048,128]{2,1,0:T(8,128)(2,1)S(1)}, u32[]{:S(2)}, u32[]{:S(2)}) collective-permute-start(bf16[3,2048,128]{2,1,0:T(8,128)(2,1)} %param.4), channel_id=1, source_target_pairs={{0,16},{8,24},{16,0},{24,8},{1,17},{9,25},{17,1},{25,9},{2,18},{10... | collective-permute-start | bytes 4718600 | tf_op jit(solution)/shard_map/ppermute | solution.py:37
  11.4 1.0 collective-permute-start
  12.3 33.4 %collective-permute-done.1 = bf16[3,2048,128]{2,1,0:T(8,128)(2,1)S(1)} collective-permute-done((bf16[3,2048,128]{2,1,0:T(8,128)(2,1)}, bf16[3,2048,128]{2,1,0:T(8,128)(2,1)S(1)}, u32[]{:S(2)}, u32[]{:S(2)}) %collective-permute-start.1) | collective-permute-done | bytes 1572896 | tf_op jit(solution)/shard_map/ppermute | solution.py:37
  45.7 1.2 collective-permute-start.2
  46.9 0.9 exp.3
  49.2 35.8 %all-gather.2.cloned.1.call-done = bf16[8,128,2048]{2,1,0:T(8,128)(2,1)} async-done(((bf16[1,128,2048]{2,1,0:T(8,128)(2,1)}), bf16[8,128,2048]{2,1,0:T(8,128)(2,1)}) %all-gather.2.cloned.1.call-update) | async-done | bytes 4194320 | tf_op jit(solution)/shard_map/all_gather | solution.py:49
  85.0 1.9 %collective-permute-start.3 = (bf16[8,128,2048]{2,1,0:T(8,128)(2,1)}, bf16[8,128,2048]{2,1,0:T(8,128)(2,1)}, u32[]{:S(2)}, u32[]{:S(2)}) collective-permute-start(bf16[8,128,2048]{2,1,0:T(8,128)(2,1)} %all-gather.2.cloned.1.call-done), channel_id=1, source_target_pairs={{0,8},{8,0},{16,24},{24,16},{1,9},{9,1},{17,25},{25,17},{2,10},{10... | collective-permute-start | bytes 12582920 | tf_op jit(solution)/shard_map/ppermute | solution.py:37
  86.9 5.8 %pad_maximum_fusion = bf16[12,2048,128]{2,1,0:T(8,128)(2,1)} fusion(bf16[3,2048,128]{2,1,0:T(8,128)(2,1)} %collective-permute-done.2, bf16[3,2048,128]{2,1,0:T(8,128)(2,1)S(1)} %collective-permute-done.1, bf16[3,2048,128]{2,1,0:T(8,128)(2,1)} %collective-permute-done, bf16[3,2048,128]{2,1,0:T(8,128)(2,1)} %param.4), kind=kLoop, calls=%fused_computation.2 | loop fusion | flops 9437184 | bytes 12582912 | tf_op jit(solution)/shard_map/concatenate | solution.py:54
  92.7 5.5 %gather_fusion = bf16[6,2048,128]{2,1,0:T(8,128)(2,1)} fusion(bf16[12,2048,128]{2,1,0:T(8,128)(2,1)} %pad_maximum_fusion, s32[1024]{0:T(1024)S(1)} %pad_clamp_fusion), kind=kCustom, calls=%fused_computation | custom fusion | bytes 6291480 | tf_op jit(solution)/shard_map/gather | solution.py:59
  98.2 5.1 %broadcast_select_fusion = (bf16[6,2048,128]{2,1,0:T(8,128)(2,1)}, bf16[6,2048,128]{2,1,0:T(8,128)(2,1)S(1)}) fusion(pred[6]{0:T(512)(128)(4,1)S(1)} %broadcast_compare_fusion, bf16[6,2048,128]{2,1,0:T(8,128)(2,1)} %gather_fusion, f32[6,2048]{1,0:T(8,128)S(1)} %exp.3), kind=kLoop, calls=%fused_computation.19 | loop fusion | flops 6291456 | bytes 9486342 | tf_op jit(solution)/shard_map/jit(_where)/select_n | solution.py:60
  103.3 1.7 %copy-done.1 = bf16[6,2048,128]{2,1,0:T(8,128)(2,1)} copy-done((bf16[6,2048,128]{2,1,0:T(8,128)(2,1)}, bf16[6,2048,128]{2,1,0:T(8,128)(2,1)S(1)}, u32[]{:S(2)}) %copy-start.1) | copy-done | bytes 3145752
  105.0 4.7 %copy.26 = f32[6,128,128]{0,2,1:T(8,128)} copy(f32[6,128,128]{2,1,0:T(8,128)S(1)} %slice_convert_fusion) | data formatting | bytes 786432 | tf_op jit(solution)/shard_map/slice | solution.py:12
  109.7 1.8 %gather_fusion.1 = f32[128,6]{1,0:T(8,128)S(1)} fusion(f32[6,128,128]{0,2,1:T(8,128)} %copy.26, s32[128]{0:T(128)S(1)} %or_bitcast_fusion), kind=kCustom, calls=%fused_computation.1 | custom fusion | bytes 7168 | tf_op jit(solution)/shard_map/jit(diagonal)/gather | solution.py:14
  111.6 1.5 convolution_subtract_fusion.2
  113.6 1.3 convolution_subtract_fusion.1
  116.3 2.8 %convolution_convert_fusion = bf16[6,2048,128]{2,1,0:T(8,128)(2,1)S(1)} fusion(bf16[6,2048,128]{2,1,0:T(8,128)(2,1)S(1)} %copy-done.2, f32[6,128,128]{2,1,0:T(8,128)S(1)} %fusion.24), kind=kOutput, calls=%fused_computation.8 | convolution fusion | flops 2417491968 | bytes 6684672 | tf_op jit(solution)/shard_map/wnk,wkj->wnj/dot_general | solution.py:24
  119.1 1.7 %copy-done.3 = bf16[6,2048,128]{2,1,0:T(8,128)(2,1)} copy-done((bf16[6,2048,128]{2,1,0:T(8,128)(2,1)}, bf16[6,2048,128]{2,1,0:T(8,128)(2,1)S(1)}, u32[]{:S(2)}) %copy-start.3) | copy-done | bytes 3145752
  120.8 5.1 %fusion.2 = f32[6,128,8,128]{3,1,2,0:T(8,128)} fusion(bf16[8,128,2048]{2,1,0:T(8,128)(2,1)S(1)} %copy-done.5, bf16[6,2048,128]{2,1,0:T(8,128)(2,1)S(1)} %convolution_convert_fusion), kind=kOutput, calls=%fused_computation.6 | convolution fusion | flops 3221225472 | bytes 10485760 | tf_op jit(solution)/shard_map/gin,wnj->wgij/dot_general | solution.py:29
  125.9 3.6 %copy.29 = f32[6,128,8,128]{1,3,2,0:T(8,128)} copy(f32[6,128,8,128]{3,1,2,0:T(8,128)} %fusion.2) | data formatting | bytes 6291456 | tf_op jit(solution)/shard_map/gin,wnj->wgij/dot_general | solution.py:29
  129.5 7.4 %fusion = f32[6,128,8,128]{3,1,2,0:T(8,128)} fusion(bf16[8,128,2048]{2,1,0:T(8,128)(2,1)} %collective-permute-done.3, bf16[6,2048,128]{2,1,0:T(8,128)(2,1)} %copy-done.3), kind=kOutput, calls=%fused_computation.4 | convolution fusion | flops 3221225472 | bytes 10485760 | tf_op jit(solution)/shard_map/gin,wnj->wgij/dot_general | solution.py:29
  136.9 3.5 %copy.31 = f32[6,128,8,128]{1,3,2,0:T(8,128)} copy(f32[6,128,8,128]{3,1,2,0:T(8,128)} %fusion) | data formatting | bytes 6291456 | tf_op jit(solution)/shard_map/gin,wnj->wgij/dot_general | solution.py:29
  140.4 5.9 %fusion.7 = (f32[6,8]{1,0:T(8,128)S(1)}, f32[6,8]{1,0:T(8,128)S(1)}, f32[6,8]{1,0:T(8,128)S(1)}, f32[6,8]{1,0:T(8,128)S(1)}) fusion(f32[6,128,8,128]{1,3,2,0:T(8,128)} %copy.31, pred[128,128]{1,0:T(8,128)(4,1)S(1)} %iota_compare_fusion.1, f32[6,128,8,128]{3,1,2,0:T(8,128)} %fusion, f32[6,128,8,128]{3,1,2,0:T(8,128)} %fusion.2, f32[6,128,8,128]{1,3,2,0:T(8,128)} %copy.29), kind=kLoop, calls=%fused_computation.14 | loop fusion | flops 6291264 | bytes 12600064 | tf_op jit(solution)/shard_map/wgii->wg/reduce_sum | solution.py:30
  (29 shorter events, 4.2 us)
Async XLA Ops:
  7.2 1.2 copy-start
  7.2 77.9 %all-gather.2.cloned.1.call-start = ((), (), s32[]{:S(2)}) async-start(), calls=%async_computation | async-start | bytes 4718592 | tf_op jit(solution)/shard_map/all_gather | solution.py:49
  9.3 36.4 %collective-permute-start.1 = (bf16[3,2048,128]{2,1,0:T(8,128)(2,1)}, bf16[3,2048,128]{2,1,0:T(8,128)(2,1)S(1)}, u32[]{:S(2)}, u32[]{:S(2)}) collective-permute-start(bf16[3,2048,128]{2,1,0:T(8,128)(2,1)} %param.4), channel_id=1, source_target_pairs={{0,16},{8,24},{16,0},{24,8},{1,17},{9,25},{17,1},{25,9},{2,18},{10... | collective-permute-start | bytes 4718600 | tf_op jit(solution)/shard_map/ppermute | solution.py:37
  11.4 75.5 %collective-permute-start = (bf16[3,2048,128]{2,1,0:T(8,128)(2,1)}, bf16[3,2048,128]{2,1,0:T(8,128)(2,1)}, u32[]{:S(2)}, u32[]{:S(2)}) collective-permute-start(bf16[3,2048,128]{2,1,0:T(8,128)(2,1)} %param.4), channel_id=1, source_target_pairs={{0,8},{8,0},{16,24},{24,16},{1,9},{9,1},{17,25},{25,17},{2,10},{10... | collective-permute-start | bytes 4718600 | tf_op jit(solution)/shard_map/ppermute | solution.py:37
  45.7 41.2 %collective-permute-start.2 = (bf16[3,2048,128]{2,1,0:T(8,128)(2,1)S(1)}, bf16[3,2048,128]{2,1,0:T(8,128)(2,1)}, u32[]{:S(2)}, u32[]{:S(2)}) collective-permute-start(bf16[3,2048,128]{2,1,0:T(8,128)(2,1)S(1)} %collective-permute-done.1), channel_id=1, source_target_pairs={{0,8},{8,0},{16,24},{24,16},{1,9},{9,1},{17,25},{25,17},{2,10},{10... | collective-permute-start | bytes 4718600 | tf_op jit(solution)/shard_map/ppermute | solution.py:37
  85.0 44.5 %collective-permute-start.3 = (bf16[8,128,2048]{2,1,0:T(8,128)(2,1)}, bf16[8,128,2048]{2,1,0:T(8,128)(2,1)}, u32[]{:S(2)}, u32[]{:S(2)}) collective-permute-start(bf16[8,128,2048]{2,1,0:T(8,128)(2,1)} %all-gather.2.cloned.1.call-done), channel_id=1, source_target_pairs={{0,8},{8,0},{16,24},{24,16},{1,9},{9,1},{17,25},{25,17},{2,10},{10... | collective-permute-start | bytes 12582920 | tf_op jit(solution)/shard_map/ppermute | solution.py:37
  103.3 1.7 %copy-start.1 = (bf16[6,2048,128]{2,1,0:T(8,128)(2,1)}, bf16[6,2048,128]{2,1,0:T(8,128)(2,1)S(1)}, u32[]{:S(2)}) copy-start(bf16[6,2048,128]{2,1,0:T(8,128)(2,1)S(1)} %get-tuple-element.11) | copy-start | bytes 9437188
  111.6 3.9 %copy-start.2 = (bf16[6,2048,128]{2,1,0:T(8,128)(2,1)S(1)}, bf16[6,2048,128]{2,1,0:T(8,128)(2,1)}, u32[]{:S(2)}) copy-start(bf16[6,2048,128]{2,1,0:T(8,128)(2,1)} %copy-done.1) | copy-start | bytes 9437188
  116.3 4.5 %copy-start.5 = (bf16[8,128,2048]{2,1,0:T(8,128)(2,1)S(1)}, bf16[8,128,2048]{2,1,0:T(8,128)(2,1)}, u32[]{:S(2)}) copy-start(bf16[8,128,2048]{2,1,0:T(8,128)(2,1)} %all-gather.2.cloned.1.call-done) | copy-start | bytes 12582916
  119.1 1.7 %copy-start.3 = (bf16[6,2048,128]{2,1,0:T(8,128)(2,1)}, bf16[6,2048,128]{2,1,0:T(8,128)(2,1)S(1)}, u32[]{:S(2)}) copy-start(bf16[6,2048,128]{2,1,0:T(8,128)(2,1)S(1)} %convolution_convert_fusion) | copy-start | bytes 9437188
  140.4 6.1 %copy-start.4 = (s32[6]{0:T(128)S(1)}, s32[6]{0:T(128)}, u32[]{:S(2)}) copy-start(s32[6]{0:T(128)} %param.6) | copy-start | bytes 76
Sparse Core Ops, SparseCore 0:
  10.7 74.2 all-gather.1
where the time goes:
time: 154 us
  waiting for transfers between devices  69.2 us (45%)
  local copies, waits for them, and re-layouts  25.4 us (16%)
  matrix products  20 us (13%)
  other arithmetic  18.9 us (12%)
  between operations  14.2 us (9%)
  starting transfers between devices  6.19 us (4%)
    all_gather x1, waiting for transfers between devices, body(): gathered = lax.all_gather(mine, 'chol', axis=0, tiled=True)  35.8 us
    ppermute x4, waiting for transfers between devices, swap_pairs(): return lax.ppermute(x, axis, perm)  33.4 us
    dot_general x2, matrix products, block_energy(): jnp.einsum('gin,wnj->wgij', vectors, theta, preferred_element_type=jnp.fl...  12.5 us
    dot_general x2, local copies, waits for them, and re-layouts, block_energy(): jnp.einsum('gin,wnj->wgij', vectors, theta, preferred_element_type=jnp.fl...  7.09 us
    ppermute x4, starting transfers between devices, swap_pairs(): return lax.ppermute(x, axis, perm)  6.15 us
    reduce_sum x1, other arithmetic, block_energy(): traces = jnp.einsum('wgii->wg', blocks)  5.93 us
    concatenate x1, other arithmetic, body(): jnp.concatenate([old_walkers, beside, across, diagonal_peer], axis=0)  5.83 us
    gather x1, local copies, waits for them, and re-layouts, body(): column[index].astype(jnp.float32)  5.5 us
  transfers between devices with their start and end apart: 5, of which 2 were waited for; matrix products, arithmetic and copies ran while one was open for 27% of the time, Pallas kernels for 0%

commit v1 on v0

--- a/solution.py
+++ b/solution.py
@@ -46,7 +46,12 @@
     local_g = half_chol.shape[0]
     half_g = local_g // 2
     mine = lax.dynamic_slice_in_dim(half_chol, core * half_g, half_g, axis=0)
-    gathered = lax.all_gather(mine, "chol", axis=0, tiled=True)
+    ring = [mine]
+    for hop in range(7):
+        ring.append(lax.ppermute(ring[-1], "chol", [(dev, (dev + 1) % 8) for dev in range(8)]))
+    gathered = jnp.roll(
+        jnp.concatenate(ring[::-1], axis=0), (lax.axis_index("chol") + 1) * ring[0].shape[0], axis=0
+    )
     other = swap_pairs(gathered, "walk", n_walk, 1)
     across = swap_pairs(old_walkers, "walk", n_walk, 2)
     beside = swap_pairs(old_walkers, "walk", n_walk, 1)

time: 154 us -> 168 us (1.091)
  between operations: 14.2 us -> 0.91 us
  starting transfers between devices: 6.19 us -> 17 us
  waiting for transfers between devices: 69.2 us -> 79.3 us
  local copies, waits for them, and re-layouts: 25.4 us -> 28.9 us
  matrix products: 20 us -> 21.7 us
    ppermute x0 -> x7, waiting for transfers between devices: none -> 72.7 us  [body(): lax.ppermute(ring[-1], 'chol', [(dev, (dev + 1) % 8) for dev in range(8)])]
    all_gather x1 -> x0, waiting for transfers between devices: 35.8 us -> none  [body(): gathered = lax.all_gather(mine, 'chol', axis=0, tiled=True)]
    ppermute x4, waiting for transfers between devices: 33.4 us -> 6.54 us  [swap_pairs(): return lax.ppermute(x, axis, perm)]
    ppermute x4, starting transfers between devices: 6.15 us -> 14.9 us  [swap_pairs(): return lax.ppermute(x, axis, perm)]
    dynamic_slice x0 -> x1, local copies, waits for them, and re-layouts: none -> 2.29 us  [body(): jnp.roll(jnp.concatenate(ring[::-1], axis=0), (lax.axis_index('chol') + 1...]
    ppermute x0 -> x7, starting transfers between devices: none -> 2.14 us  [body(): lax.ppermute(ring[-1], 'chol', [(dev, (dev + 1) % 8) for dev in range(8)])]
    unnamed x12 -> x25, local copies, waits for them, and re-layouts: 4.49 us -> 6.47 us
  transfers between devices with their start and end apart: 5 -> 11, of which waited for: 2 -> 7; matrix products, arithmetic and copies ran while one was open for 27% -> 30% of each run, Pallas kernels for 0% -> 0%
where the time goes in v1:
time: 168 us; the launch traced here: 167 us
  waiting for transfers between devices  79.3 us (47%)
  local copies, waits for them, and re-layouts  28.9 us (17%)
  matrix products  21.7 us (13%)
  other arithmetic  19.3 us (11%)
  starting transfers between devices  17 us (10%)
    ppermute x7, waiting for transfers between devices, body(): lax.ppermute(ring[-1], 'chol', [(dev, (dev + 1) % 8) for dev in range(8)])  72.7 us
    ppermute x4, starting transfers between devices, swap_pairs(): return lax.ppermute(x, axis, perm)  14.9 us
    dot_general x2, matrix products, block_energy(): jnp.einsum('gin,wnj->wgij', vectors, theta, preferred_element_type=jnp.fl...  12.8 us
    ppermute x4, waiting for transfers between devices, swap_pairs(): return lax.ppermute(x, axis, perm)  6.54 us
    unnamed x25, local copies, waits for them, and re-layouts  6.47 us
    dot_general x2, local copies, waits for them, and re-layouts, block_energy(): jnp.einsum('gin,wnj->wgij', vectors, theta, preferred_element_type=jnp.fl...  5.99 us
    gather x1, local copies, waits for them, and re-layouts, body(): column[index].astype(jnp.float32)  5.5 us
    concatenate x1, other arithmetic, body(): jnp.concatenate([old_walkers, beside, across, diagonal_peer], axis=0)  5.29 us
  transfers between devices with their start and end apart: 11, of which 7 were waited for; matrix products, arithmetic and copies ran while one was open for 30% of the time, Pallas kernels for 0%

profile of v1, /device:TPU:1, one launch (start us, length us, event | category | flops | bytes accessed | tf_op | source)
XLA Modules:
  0.0 167.0 jit_solution(15794823494766441189)
XLA Ops:
  1.8 2.1 %collective-permute-start.3 = (bf16[1,128,2048]{2,1,0:T(8,128)(2,1)S(1)}, bf16[1,128,2048]{2,1,0:T(8,128)(2,1)S(1)}, u32[]{:S(2)}, u32[]{:S(2)}) collective-permute-start(bf16[1,128,2048]{2,1,0:T(8,128)(2,1)S(1)} %constant_dynamic-slice_fusion.1), channel_id=1, source_target_pairs={{0,1},{1,2},{2,3},{3,4},{4,5},{5,6},{6,7},{7,0},{8,9},{9,10},{10,1... | collective-permute-start | bytes 1572872 | tf_op jit(solution)/shard_map/ppermute | solution.py:51
  3.9 14.7 %collective-permute-done.3 = bf16[1,128,2048]{2,1,0:T(8,128)(2,1)S(1)} collective-permute-done((bf16[1,128,2048]{2,1,0:T(8,128)(2,1)S(1)}, bf16[1,128,2048]{2,1,0:T(8,128)(2,1)S(1)}, u32[]{:S(2)}, u32[]{:S(2)}) %collective-permute-start.3) | collective-permute-done | bytes 524320 | tf_op jit(solution)/shard_map/ppermute | solution.py:51
  18.6 14.9 %collective-permute-done.4 = bf16[1,128,2048]{2,1,0:T(8,128)(2,1)S(1)} collective-permute-done((bf16[1,128,2048]{2,1,0:T(8,128)(2,1)S(1)}, bf16[1,128,2048]{2,1,0:T(8,128)(2,1)S(1)}, u32[]{:S(2)}, u32[]{:S(2)}) %collective-permute-start.4) | collective-permute-done | bytes 524320 | tf_op jit(solution)/shard_map/ppermute | solution.py:51
  33.5 14.0 %collective-permute-done.5 = bf16[1,128,2048]{2,1,0:T(8,128)(2,1)S(1)} collective-permute-done((bf16[1,128,2048]{2,1,0:T(8,128)(2,1)S(1)}, bf16[1,128,2048]{2,1,0:T(8,128)(2,1)S(1)}, u32[]{:S(2)}, u32[]{:S(2)}) %collective-permute-start.5) | collective-permute-done | bytes 524320 | tf_op jit(solution)/shard_map/ppermute | solution.py:51
  47.5 13.0 %collective-permute-done.6 = bf16[1,128,2048]{2,1,0:T(8,128)(2,1)S(1)} collective-permute-done((bf16[1,128,2048]{2,1,0:T(8,128)(2,1)S(1)}, bf16[1,128,2048]{2,1,0:T(8,128)(2,1)S(1)}, u32[]{:S(2)}, u32[]{:S(2)}) %collective-permute-start.6) | collective-permute-done | bytes 524320 | tf_op jit(solution)/shard_map/ppermute | solution.py:51
  61.0 11.7 %collective-permute-done.7 = bf16[1,128,2048]{2,1,0:T(8,128)(2,1)} collective-permute-done((bf16[1,128,2048]{2,1,0:T(8,128)(2,1)S(1)}, bf16[1,128,2048]{2,1,0:T(8,128)(2,1)}, u32[]{:S(2)}, u32[]{:S(2)}) %collective-permute-start.7) | collective-permute-done | bytes 524320 | tf_op jit(solution)/shard_map/ppermute | solution.py:51
  72.8 4.9 %collective-permute-start = (bf16[3,2048,128]{2,1,0:T(8,128)(2,1)}, bf16[3,2048,128]{2,1,0:T(8,128)(2,1)}, u32[]{:S(2)}, u32[]{:S(2)}) collective-permute-start(bf16[3,2048,128]{2,1,0:T(8,128)(2,1)} %param.4), channel_id=1, source_target_pairs={{0,8},{8,0},{16,24},{24,16},{1,9},{9,1},{17,25},{25,17},{2,10},{10... | collective-permute-start | bytes 4718600 | tf_op jit(solution)/shard_map/ppermute | solution.py:37
  79.8 4.4 %collective-permute-done.8 = bf16[1,128,2048]{2,1,0:T(8,128)(2,1)} collective-permute-done((bf16[1,128,2048]{2,1,0:T(8,128)(2,1)}, bf16[1,128,2048]{2,1,0:T(8,128)(2,1)}, u32[]{:S(2)}, u32[]{:S(2)}) %collective-permute-start.8) | collective-permute-done | bytes 524320 | tf_op jit(solution)/shard_map/ppermute | solution.py:51
  86.2 6.5 %collective-permute-done.1 = bf16[3,2048,128]{2,1,0:T(8,128)(2,1)} collective-permute-done((bf16[3,2048,128]{2,1,0:T(8,128)(2,1)}, bf16[3,2048,128]{2,1,0:T(8,128)(2,1)}, u32[]{:S(2)}, u32[]{:S(2)}) %collective-permute-start.1) | collective-permute-done | bytes 1572896 | tf_op jit(solution)/shard_map/ppermute | solution.py:37
  92.7 4.9 %collective-permute-start.2 = (bf16[3,2048,128]{2,1,0:T(8,128)(2,1)}, bf16[3,2048,128]{2,1,0:T(8,128)(2,1)S(1)}, u32[]{:S(2)}, u32[]{:S(2)}) collective-permute-start(bf16[3,2048,128]{2,1,0:T(8,128)(2,1)} %collective-permute-done.1), channel_id=1, source_target_pairs={{0,8},{8,0},{16,24},{24,16},{1,9},{9,1},{17,25},{25,17},{2,10},{10... | collective-permute-start | bytes 4718600 | tf_op jit(solution)/shard_map/ppermute | solution.py:37
  102.6 2.3 %constant_dynamic-slice_fusion = bf16[8,128,2048]{2,1,0:T(8,128)(2,1)} fusion(bf16[16,128,2048]{2,1,0:T(8,128)(2,1)S(1)} %constant_dynamic-update-slice_fusion, s32[]{:T(128)S(6)} %select_n.61), kind=kLoop, calls=%fused_computation.63 | loop fusion | bytes 8388612 | tf_op jit(solution)/shard_map/jit(_roll_dynamic)/dynamic_slice | solution.py:52
  104.9 4.5 %collective-permute-start.10 = (bf16[8,128,2048]{2,1,0:T(8,128)(2,1)}, bf16[8,128,2048]{2,1,0:T(8,128)(2,1)}, u32[]{:S(2)}, u32[]{:S(2)}) collective-permute-start(bf16[8,128,2048]{2,1,0:T(8,128)(2,1)} %constant_dynamic-slice_fusion), channel_id=1, source_target_pairs={{0,8},{8,0},{16,24},{24,16},{1,9},{9,1},{17,25},{25,17},{2,10},{10... | collective-permute-start | bytes 12582920 | tf_op jit(solution)/shard_map/ppermute | solution.py:37
  109.4 5.3 %pad_maximum_fusion = bf16[12,2048,128]{2,1,0:T(8,128)(2,1)} fusion(bf16[3,2048,128]{2,1,0:T(8,128)(2,1)S(1)} %collective-permute-done.2, bf16[3,2048,128]{2,1,0:T(8,128)(2,1)} %collective-permute-done.1, bf16[3,2048,128]{2,1,0:T(8,128)(2,1)} %collective-permute-done, bf16[3,2048,128]{2,1,0:T(8,128)(2,1)S(1)} %copy-done.2), kind=kLoop, calls=%fused_computation.2 | loop fusion | flops 9437184 | bytes 12582912 | tf_op jit(solution)/shard_map/concatenate | solution.py:59
  114.7 5.5 %gather_fusion = bf16[6,2048,128]{2,1,0:T(8,128)(2,1)} fusion(bf16[12,2048,128]{2,1,0:T(8,128)(2,1)} %pad_maximum_fusion, s32[1024]{0:T(1024)S(1)} %pad_clamp_fusion), kind=kCustom, calls=%fused_computation | custom fusion | bytes 6291480 | tf_op jit(solution)/shard_map/gather | solution.py:64
  120.2 5.1 %broadcast_select_fusion = (bf16[6,2048,128]{2,1,0:T(8,128)(2,1)}, bf16[6,2048,128]{2,1,0:T(8,128)(2,1)S(1)}) fusion(pred[6]{0:T(512)(128)(4,1)S(1)} %broadcast_compare_fusion, bf16[6,2048,128]{2,1,0:T(8,128)(2,1)} %gather_fusion, f32[6,2048]{1,0:T(8,128)S(1)} %exp.3), kind=kLoop, calls=%fused_computation.19 | loop fusion | flops 6291456 | bytes 9486342 | tf_op jit(solution)/shard_map/jit(_where)/select_n | solution.py:65
  125.3 4.7 %copy.20 = f32[6,128,128]{0,2,1:T(8,128)} copy(f32[6,128,128]{2,1,0:T(8,128)S(1)} %slice_convert_fusion) | data formatting | bytes 786432 | tf_op jit(solution)/shard_map/slice | solution.py:12
  130.0 1.8 %gather_fusion.1 = f32[128,6]{1,0:T(8,128)S(1)} fusion(f32[6,128,128]{0,2,1:T(8,128)} %copy.20, s32[128]{0:T(128)S(1)} %or_bitcast_fusion), kind=kCustom, calls=%fused_computation.1 | custom fusion | bytes 7168 | tf_op jit(solution)/shard_map/jit(diagonal)/gather | solution.py:14
  137.9 2.8 %convolution_convert_fusion = bf16[6,2048,128]{2,1,0:T(8,128)(2,1)S(1)} fusion(bf16[6,2048,128]{2,1,0:T(8,128)(2,1)S(1)} %get-tuple-element.11, f32[6,128,128]{2,1,0:T(8,128)S(1)} %fusion.24), kind=kOutput, calls=%fused_computation.8 | convolution fusion | flops 2417491968 | bytes 6684672 | tf_op jit(solution)/shard_map/wnk,wkj->wnj/dot_general | solution.py:24
  140.8 1.7 %copy-done = bf16[6,2048,128]{2,1,0:T(8,128)(2,1)} copy-done((bf16[6,2048,128]{2,1,0:T(8,128)(2,1)}, bf16[6,2048,128]{2,1,0:T(8,128)(2,1)S(1)}, u32[]{:S(2)}) %copy-start) | copy-done | bytes 3145752
  142.5 5.3 %fusion.2 = f32[6,128,8,128]{3,1,2,0:T(8,128)S(1)} fusion(bf16[8,128,2048]{2,1,0:T(8,128)(2,1)} %constant_dynamic-slice_fusion, bf16[6,2048,128]{2,1,0:T(8,128)(2,1)S(1)} %convolution_convert_fusion), kind=kOutput, calls=%fused_computation.6 | convolution fusion | flops 3221225472 | bytes 10485760 | tf_op jit(solution)/shard_map/gin,wnj->wgij/dot_general | solution.py:29
  147.8 2.4 %copy.23 = f32[6,128,8,128]{1,3,2,0:T(8,128)} copy(f32[6,128,8,128]{3,1,2,0:T(8,128)S(1)} %fusion.2) | data formatting | bytes 6291456 | tf_op jit(solution)/shard_map/gin,wnj->wgij/dot_general | solution.py:29
  150.3 7.5 %fusion = f32[6,128,8,128]{3,1,2,0:T(8,128)} fusion(bf16[8,128,2048]{2,1,0:T(8,128)(2,1)} %collective-permute-done.10, bf16[6,2048,128]{2,1,0:T(8,128)(2,1)} %copy-done), kind=kOutput, calls=%fused_computation.4 | convolution fusion | flops 3221225472 | bytes 10485760 | tf_op jit(solution)/shard_map/gin,wnj->wgij/dot_general | solution.py:29
  157.7 3.5 %copy.25 = f32[6,128,8,128]{1,3,2,0:T(8,128)} copy(f32[6,128,8,128]{3,1,2,0:T(8,128)} %fusion) | data formatting | bytes 6291456 | tf_op jit(solution)/shard_map/gin,wnj->wgij/dot_general | solution.py:29
  161.3 5.0 %fusion.7 = (f32[6,8]{1,0:T(8,128)S(1)}, f32[6,8]{1,0:T(8,128)S(1)}, f32[6,8]{1,0:T(8,128)S(1)}, f32[6,8]{1,0:T(8,128)S(1)}) fusion(f32[6,128,8,128]{1,3,2,0:T(8,128)} %copy.25, pred[128,128]{1,0:T(8,128)(4,1)S(1)} %copy-done.3, f32[6,128,8,128]{3,1,2,0:T(8,128)} %fusion, f32[6,128,8,128]{3,1,2,0:T(8,128)S(1)} %fusion.2, f32[6,128,8,128]{1,3,2,0:T(8,128)} %copy.23), kind=kLoop, calls=%fused_computation.14 | loop fusion | flops 6291264 | bytes 12600064 | tf_op jit(solution)/shard_map/wgii->wg/reduce_sum | solution.py:30
  (55 shorter events, 17.4 us)
Async XLA Ops:
  0.6 99.4 %copy-start.1 = (bf16[2,128,2048]{2,1,0:T(8,128)(2,1)S(1)}, bf16[2,128,2048]{2,1,0:T(8,128)(2,1)}, u32[]{:S(2)}) copy-start(bf16[2,128,2048]{2,1,0:T(8,128)(2,1)} %param.5) | copy-start | bytes 3145732
  1.8 16.8 %collective-permute-start.3 = (bf16[1,128,2048]{2,1,0:T(8,128)(2,1)S(1)}, bf16[1,128,2048]{2,1,0:T(8,128)(2,1)S(1)}, u32[]{:S(2)}, u32[]{:S(2)}) collective-permute-start(bf16[1,128,2048]{2,1,0:T(8,128)(2,1)S(1)} %constant_dynamic-slice_fusion.1), channel_id=1, source_target_pairs={{0,1},{1,2},{2,3},{3,4},{4,5},{5,6},{6,7},{7,0},{8,9},{9,10},{10,1... | collective-permute-start | bytes 1572872 | tf_op jit(solution)/shard_map/ppermute | solution.py:51
  18.6 14.9 %collective-permute-start.4 = (bf16[1,128,2048]{2,1,0:T(8,128)(2,1)S(1)}, bf16[1,128,2048]{2,1,0:T(8,128)(2,1)S(1)}, u32[]{:S(2)}, u32[]{:S(2)}) collective-permute-start(bf16[1,128,2048]{2,1,0:T(8,128)(2,1)S(1)} %collective-permute-done.3), channel_id=1, source_target_pairs={{0,1},{1,2},{2,3},{3,4},{4,5},{5,6},{6,7},{7,0},{8,9},{9,10},{10,1... | collective-permute-start | bytes 1572872 | tf_op jit(solution)/shard_map/ppermute | solution.py:51
  33.5 14.0 %collective-permute-start.5 = (bf16[1,128,2048]{2,1,0:T(8,128)(2,1)S(1)}, bf16[1,128,2048]{2,1,0:T(8,128)(2,1)S(1)}, u32[]{:S(2)}, u32[]{:S(2)}) collective-permute-start(bf16[1,128,2048]{2,1,0:T(8,128)(2,1)S(1)} %collective-permute-done.4), channel_id=1, source_target_pairs={{0,1},{1,2},{2,3},{3,4},{4,5},{5,6},{6,7},{7,0},{8,9},{9,10},{10,1... | collective-permute-start | bytes 1572872 | tf_op jit(solution)/shard_map/ppermute | solution.py:51
  47.5 13.0 %collective-permute-start.6 = (bf16[1,128,2048]{2,1,0:T(8,128)(2,1)S(1)}, bf16[1,128,2048]{2,1,0:T(8,128)(2,1)S(1)}, u32[]{:S(2)}, u32[]{:S(2)}) collective-permute-start(bf16[1,128,2048]{2,1,0:T(8,128)(2,1)S(1)} %collective-permute-done.5), channel_id=1, source_target_pairs={{0,1},{1,2},{2,3},{3,4},{4,5},{5,6},{6,7},{7,0},{8,9},{9,10},{10,1... | collective-permute-start | bytes 1572872 | tf_op jit(solution)/shard_map/ppermute | solution.py:51
  60.5 12.2 %collective-permute-start.7 = (bf16[1,128,2048]{2,1,0:T(8,128)(2,1)S(1)}, bf16[1,128,2048]{2,1,0:T(8,128)(2,1)}, u32[]{:S(2)}, u32[]{:S(2)}) collective-permute-start(bf16[1,128,2048]{2,1,0:T(8,128)(2,1)S(1)} %collective-permute-done.6), channel_id=1, source_target_pairs={{0,1},{1,2},{2,3},{3,4},{4,5},{5,6},{6,7},{7,0},{8,9},{9,10},{10,1... | collective-permute-start | bytes 1572872 | tf_op jit(solution)/shard_map/ppermute | solution.py:51
  60.5 32.2 %collective-permute-start.1 = (bf16[3,2048,128]{2,1,0:T(8,128)(2,1)}, bf16[3,2048,128]{2,1,0:T(8,128)(2,1)}, u32[]{:S(2)}, u32[]{:S(2)}) collective-permute-start(bf16[3,2048,128]{2,1,0:T(8,128)(2,1)} %param.4), channel_id=1, source_target_pairs={{0,16},{8,24},{16,0},{24,8},{1,17},{9,25},{17,1},{25,9},{2,18},{10... | collective-permute-start | bytes 4718600 | tf_op jit(solution)/shard_map/ppermute | solution.py:37
  72.8 11.5 %collective-permute-start.8 = (bf16[1,128,2048]{2,1,0:T(8,128)(2,1)}, bf16[1,128,2048]{2,1,0:T(8,128)(2,1)}, u32[]{:S(2)}, u32[]{:S(2)}) collective-permute-start(bf16[1,128,2048]{2,1,0:T(8,128)(2,1)} %collective-permute-done.7), channel_id=1, source_target_pairs={{0,1},{1,2},{2,3},{3,4},{4,5},{5,6},{6,7},{7,0},{8,9},{9,10},{10,1... | collective-permute-start | bytes 1572872 | tf_op jit(solution)/shard_map/ppermute | solution.py:51
  72.8 36.6 %collective-permute-start = (bf16[3,2048,128]{2,1,0:T(8,128)(2,1)}, bf16[3,2048,128]{2,1,0:T(8,128)(2,1)}, u32[]{:S(2)}, u32[]{:S(2)}) collective-permute-start(bf16[3,2048,128]{2,1,0:T(8,128)(2,1)} %param.4), channel_id=1, source_target_pairs={{0,8},{8,0},{16,24},{24,16},{1,9},{9,1},{17,25},{25,17},{2,10},{10... | collective-permute-start | bytes 4718600 | tf_op jit(solution)/shard_map/ppermute | solution.py:37
  84.3 13.4 %collective-permute-start.9 = (bf16[1,128,2048]{2,1,0:T(8,128)(2,1)}, bf16[1,128,2048]{2,1,0:T(8,128)(2,1)S(1)}, u32[]{:S(2)}, u32[]{:S(2)}) collective-permute-start(bf16[1,128,2048]{2,1,0:T(8,128)(2,1)} %collective-permute-done.8), channel_id=1, source_target_pairs={{0,1},{1,2},{2,3},{3,4},{4,5},{5,6},{6,7},{7,0},{8,9},{9,10},{10,1... | collective-permute-start | bytes 1572872 | tf_op jit(solution)/shard_map/ppermute | solution.py:51
  92.7 16.7 %collective-permute-start.2 = (bf16[3,2048,128]{2,1,0:T(8,128)(2,1)}, bf16[3,2048,128]{2,1,0:T(8,128)(2,1)S(1)}, u32[]{:S(2)}, u32[]{:S(2)}) collective-permute-start(bf16[3,2048,128]{2,1,0:T(8,128)(2,1)} %collective-permute-done.1), channel_id=1, source_target_pairs={{0,8},{8,0},{16,24},{24,16},{1,9},{9,1},{17,25},{25,17},{2,10},{10... | collective-permute-start | bytes 4718600 | tf_op jit(solution)/shard_map/ppermute | solution.py:37
  102.4 7.0 %copy-start.2 = (bf16[3,2048,128]{2,1,0:T(8,128)(2,1)S(1)}, bf16[3,2048,128]{2,1,0:T(8,128)(2,1)}, u32[]{:S(2)}) copy-start(bf16[3,2048,128]{2,1,0:T(8,128)(2,1)} %param.4) | copy-start | bytes 4718596
  104.9 45.4 %collective-permute-start.10 = (bf16[8,128,2048]{2,1,0:T(8,128)(2,1)}, bf16[8,128,2048]{2,1,0:T(8,128)(2,1)}, u32[]{:S(2)}, u32[]{:S(2)}) collective-permute-start(bf16[8,128,2048]{2,1,0:T(8,128)(2,1)} %constant_dynamic-slice_fusion), channel_id=1, source_target_pairs={{0,8},{8,0},{16,24},{24,16},{1,9},{9,1},{17,25},{25,17},{2,10},{10... | collective-permute-start | bytes 12582920 | tf_op jit(solution)/shard_map/ppermute | solution.py:37
  140.8 1.7 %copy-start = (bf16[6,2048,128]{2,1,0:T(8,128)(2,1)}, bf16[6,2048,128]{2,1,0:T(8,128)(2,1)S(1)}, u32[]{:S(2)}) copy-start(bf16[6,2048,128]{2,1,0:T(8,128)(2,1)S(1)} %convolution_convert_fusion) | copy-start | bytes 9437188
  157.7 3.5 %copy-start.3 = (pred[128,128]{1,0:T(8,128)(4,1)S(1)}, pred[128,128]{1,0:T(8,128)(4,1)}, u32[]{:S(2)}) copy-start(pred[128,128]{1,0:T(8,128)(4,1)} %iota_compare_fusion.1) | copy-start | bytes 49156
  161.3 5.2 %copy-start.4 = (s32[6]{0:T(128)S(1)}, s32[6]{0:T(128)}, u32[]{:S(2)}) copy-start(s32[6]{0:T(128)} %param.6) | copy-start | bytes 76
